TPU v7x, 512 devices: a whole 4x4x16 slice. The times are simulated.
512 devices in a mesh: pair: 32 (over z_lo, y), loop: 16 (over x, z_hi, core).
Axes of the slice: x: 4, y: 4, z: 16 (z_hi: 2, z_lo: 8; z = z_hi * 8 + z_lo), core: 2. Of those that a mesh axis runs over, the one named last changes fastest.
Arguments:
- amplitudes: float32 [8192, 8192], P('pair', 'loop'), may hold values from -6 to 6
- integrals: float32 [2048, 8192], P(None, 'loop'), may hold values from -0.0625 to 0.0625
- pair_partner: int32 [8192], P('pair'), may hold values from 0 to 8191, as said below
- virtual_swap: int32 [2048], P('loop'), may hold values from 0 to 2047, as said below
Outputs:
- ladder_sym: float32 [2048, 8192], P('loop', 'pair')
Inputs may be any that keep to these rules, and one draw needn't show every extreme that they name: pair_partner[pair_partner[p]] = p, and pair_partner[p] lies in the aligned block of 256 pairs that starts 8192 / 2 pairs further on, counted modulo 8192. virtual_swap[virtual_swap[k]] = k, virtual_swap[k] != k, and virtual_swap[k] lies in the same aligned block of 64 ab pairs as k.
All inputs are finite; a program needn't handle non-finite values.
Results may differ from a plain program's by a relative error of at most 0.000071.
Values sent between devices are 32-bit elements; how exact they have to be, the bound alone decides.
No kernel may reach another device: no remote copies, remote signals or barrier semaphores. Data moves between devices by JAX's collectives and lax.ppermute only.
A program may use at most 64 MiB of HBM per device.

v0:
```python
import jax
import jax.numpy as jnp
from jax import lax
from jax.sharding import PartitionSpec as P


def shifted(x, axis, by):
    count = lax.axis_size(axis)
    return lax.ppermute(x, axis, [(i, (i + by) % count) for i in range(count)])


def local(amplitudes, integrals, pair_partner, virtual_swap):
    loop_count = lax.axis_size("loop")
    pair_count = lax.axis_size("pair")
    ab_local = integrals.shape[0] // loop_count
    ij_local = amplitudes.shape[0]
    slab = lax.all_to_all(integrals, "loop", split_axis=0, concat_axis=1, tiled=True)
    ladder = lax.dot_general(
        slab,
        lax.all_gather(amplitudes, "loop", axis=1, tiled=True),
        (((1,), (1,)), ((), ())),
        precision=lax.Precision.HIGHEST,
        preferred_element_type=jnp.float32,
    )
    mirror = shifted(ladder, "pair", pair_count // 2)
    swap_local = virtual_swap - lax.axis_index("loop") * ab_local
    partner_local = pair_partner % ij_local
    mirror = jnp.take(jnp.take(mirror, swap_local, axis=0), partner_local, axis=1)
    return ladder + mirror


def solution(mesh):
    in_specs = (P("pair", "loop"), P(None, "loop"), P("pair"), P("loop"))
    out_specs = P("loop", "pair")
    return jax.shard_map(local, mesh=mesh, in_specs=in_specs, out_specs=out_specs, check_vma=False)
```

profile of v0, /device:TPU:1, one launch (start us, length us, event | category | flops | bytes accessed | tf_op | source)
XLA Modules:
  0.0 387.8 jit_solution(8886406078017381639)
XLA Ops:
  6.5 0.0 copy-start.1
  6.5 0.0 copy-start
  6.5 19.2 %all-to-all-start = ((f32[16,128,512]{2,1,0:T(8,128)}), f32[16,128,512]{2,1,0:T(8,128)}, u32[]{:S(2)}, u32[]{:S(2)}) async-start(f32[16,128,512]{2,1,0:T(8,128)} %bitcast.8), calls=%async_computation | async-start | bytes 8388608 | tf_op jit(solution)/shard_map/all_to_all | solution.py:17
  25.7 0.0 all-gather.2.cloned.1.call-start
  25.8 0.7 all-gather.2.cloned.1.call-update
  26.5 0.0 copy-done.1
  26.5 0.0 copy-done
  26.5 115.3 %all-to-all-done = f32[16,128,512]{2,1,0:T(8,128)} async-done(((f32[16,128,512]{2,1,0:T(8,128)}), f32[16,128,512]{2,1,0:T(8,128)}, u32[]{:S(2)}, u32[]{:S(2)}) %all-to-all-start) | async-done | bytes 4194336 | tf_op jit(solution)/shard_map/all_to_all | solution.py:17
  141.8 5.3 %copy.9 = f32[128,16,512]{0,2,1:T(8,128)} copy(f32[128,16,512]{2,0,1:T(8,128)} %bitcast.1) | data formatting | bytes 8388608 | tf_op jit(solution)/shard_map/all_to_all | solution.py:17
  147.1 166.5 %all-gather.2.cloned.1.call-done = f32[256,8192]{1,0:T(8,128)} async-done(((f32[256,512]{1,0:T(8,128)}), f32[256,8192]{1,0:T(8,128)}) %all-gather.2.cloned.1.call-update) | async-done | bytes 8388624 | tf_op jit(solution)/shard_map/all_gather | solution.py:20
  313.6 11.4 %fusion.1 = f32[128,256]{1,0:T(8,128)S(1)} fusion(f32[128,8192]{0,1:T(8,128)} %bitcast.7, f32[256,8192]{1,0:T(8,128)} %all-gather.2.cloned.1.call-done), kind=kOutput, calls=%fused_computation.14 | convolution fusion | flops 3221225472 | bytes 12713984 | tf_op jit(solution)/shard_map/dot_general | solution.py:18
  325.0 49.9 %collective-permute-start = (f32[128,256]{1,0:T(8,128)S(1)}, f32[128,256]{1,0:T(8,128)S(1)}, u32[]{:S(2)}, u32[]{:S(2)}) collective-permute-start(f32[128,256]{1,0:T(8,128)S(1)} %fusion.1), channel_id=1, source_target_pairs={{0,256},{16,272},{32,288},{48,304},{64,320},{80,336},{96,352},{112... | collective-permute-start | bytes 393224 | tf_op jit(solution)/shard_map/ppermute | solution.py:9
  374.9 3.5 collective-permute-done
  378.5 0.8 gather_fusion
  379.2 0.1 broadcast_select_fusion
  379.3 0.1 copy.10
  379.4 0.7 gather_fusion.1
  380.2 0.1 copy.11
  380.3 0.7 bitcast_add_fusion
  (4 shorter events, 0.0 us)
Async XLA Ops:
  6.5 19.9 %copy-start.1 = (s32[128]{0:T(128)S(1)}, s32[128]{0:T(128)}, u32[]{:S(2)}) copy-start(s32[128]{0:T(128)} %param.7) | copy-start | bytes 1540
  6.5 20.0 %copy-start = (s32[256]{0:T(256)S(1)}, s32[256]{0:T(256)}, u32[]{:S(2)}) copy-start(s32[256]{0:T(256)} %param.6) | copy-start | bytes 3076
  6.5 135.3 %all-to-all-start = ((f32[16,128,512]{2,1,0:T(8,128)}), f32[16,128,512]{2,1,0:T(8,128)}, u32[]{:S(2)}, u32[]{:S(2)}) async-start(f32[16,128,512]{2,1,0:T(8,128)} %bitcast.8), calls=%async_computation | async-start | bytes 8388608 | tf_op jit(solution)/shard_map/all_to_all | solution.py:17
  25.7 287.9 %all-gather.2.cloned.1.call-start = ((), (), s32[]{:S(2)}) async-start(), calls=%async_computation.1 | async-start | bytes 8912896 | tf_op jit(solution)/shard_map/all_gather | solution.py:20
  325.0 53.5 %collective-permute-start = (f32[128,256]{1,0:T(8,128)S(1)}, f32[128,256]{1,0:T(8,128)S(1)}, u32[]{:S(2)}, u32[]{:S(2)}) collective-permute-start(f32[128,256]{1,0:T(8,128)S(1)} %fusion.1), channel_id=1, source_target_pairs={{0,256},{16,272},{32,288},{48,304},{64,320},{80,336},{96,352},{112... | collective-permute-start | bytes 393224 | tf_op jit(solution)/shard_map/ppermute | solution.py:9
Sparse Core Ops, SparseCore 0:
  29.9 283.7 all-gather.1
where the time goes:
time: 388 us
  waiting for transfers between devices  286 us (74%)
  starting transfers between devices  69.1 us (18%)
  between operations  13.5 us (3%)
  matrix products  11.4 us (3%)
  local copies, waits for them, and re-layouts  6.99 us (2%)
    all_gather x1, waiting for transfers between devices, local(): lax.all_gather(amplitudes, 'loop', axis=1, tiled=True)  167 us
    all_to_all x1, waiting for transfers between devices, local(): lax.all_to_all(integrals, 'loop', split_axis=0, concat_axis=1, tiled=True)  115 us
    ppermute x1, starting transfers between devices, shifted(): return lax.ppermute(x, axis, [(i, (i + by) % count) for i in range(count)])  49.9 us
    all_to_all x1, starting transfers between devices, local(): lax.all_to_all(integrals, 'loop', split_axis=0, concat_axis=1, tiled=True)  19.2 us
    dot_general x1, matrix products, local(): lax.dot_general(slab, lax.all_gather(amplitudes, 'loop', axis=1, tiled=Tr...  11.4 us
  transfers between devices with their start and end apart: 3, of which 3 were waited for; matrix products, arithmetic and copies ran while one was open for 1% of the time, Pallas kernels for 0%

commit v1 on v0

--- a/solution.py
+++ b/solution.py
@@ -15,9 +15,16 @@
     ab_local = integrals.shape[0] // loop_count
     ij_local = amplitudes.shape[0]
     slab = lax.all_to_all(integrals, "loop", split_axis=0, concat_axis=1, tiled=True)
+
+    def press_tables(inp, row_dim):
+        val2 = jax.lax.axis_size("loop")
+        long_array = jax.lax.all_to_all(jnp.stack(val2 * [inp], 0), "loop", 0, 0)
+        low = jnp.concatenate(long_array, row_dim)
+        return low
+
     ladder = lax.dot_general(
         slab,
-        lax.all_gather(amplitudes, "loop", axis=1, tiled=True),
+        press_tables(amplitudes, 1),
         (((1,), (1,)), ((), ())),
         precision=lax.Precision.HIGHEST,
         preferred_element_type=jnp.float32,

time: 388 us -> 642 us (1.65)
  the two profiles are of different devices: /device:TPU:1 before, /device:TPU:102 now
where the time goes in v1:
time: 642 us
  waiting for transfers between devices  410 us (64%)
  blocking collectives  193 us (30%)
  starting transfers between devices  19.2 us (3%)
  matrix products  13.1 us (2%)
    all_to_all x1, waiting for transfers between devices, press_tables(): long_array = jax.lax.all_to_all(jnp.stack(val2 * [inp], 0), 'loop', 0, 0)  401 us
    all_to_all x1, blocking collectives, local(): lax.all_to_all(integrals, 'loop', split_axis=0, concat_axis=1, tiled=True)  193 us
    all_to_all x1, starting transfers between devices, press_tables(): long_array = jax.lax.all_to_all(jnp.stack(val2 * [inp], 0), 'loop', 0, 0)  17.3 us
    dot_general x1, matrix products, local(): lax.dot_general(slab, press_tables(amplitudes, 1), (((1,), (1,)), ((), ()...  13.1 us
  transfers between devices with their start and end apart: 2, of which 2 were waited for; matrix products, arithmetic and copies ran while one was open for 0% of the time, Pallas kernels for 0%

profile of v1, /device:TPU:102, one launch (start us, length us, event | category | flops | bytes accessed | tf_op | source)
XLA Modules:
  0.0 641.9 jit_solution(16525026066991950324)
XLA Ops:
  0.0 0.0 copy-start
  0.0 193.0 %all_to_all.21 = f32[16,128,512]{2,1,0:T(8,128)} all-to-all(f32[16,128,512]{2,1,0:T(8,128)} %bitcast.15), channel_id=1, replica_groups=mesh['pair'=32,'loop'=16] {'loop'}, dimensions={0} | all-to-all | bytes 8388608 | tf_op jit(solution)/shard_map/all_to_all | solution.py:17
  193.0 0.0 copy-done
  193.0 4.3 stack.2
  197.3 0.0 copy-start.2
  197.3 0.0 copy-start.1
  197.3 17.3 %all-to-all-start.1 = ((f32[16,256,512]{2,1,0:T(8,128)}), f32[16,256,512]{2,1,0:T(8,128)}, u32[]{:S(2)}, u32[]{:S(2)}) async-start(f32[16,256,512]{2,1,0:T(8,128)} %stack.2), calls=%async_computation.1 | async-start | bytes 16777216 | tf_op jit(solution)/shard_map/all_to_all | solution.py:21
  214.6 0.0 copy-done.2
  214.6 0.0 copy-done.1
  214.7 400.5 %all-to-all-done.1 = f32[16,256,512]{2,1,0:T(8,128)} async-done(((f32[16,256,512]{2,1,0:T(8,128)}), f32[16,256,512]{2,1,0:T(8,128)}, u32[]{:S(2)}, u32[]{:S(2)}) %all-to-all-start.1) | async-done | bytes 8388640 | tf_op jit(solution)/shard_map/all_to_all | solution.py:21
  615.2 13.1 %fusion.3 = f32[128,256]{1,0:T(8,128)S(1)} fusion(f32[16,256,512]{2,1,0:T(8,128)} %all-to-all-done.1, f32[16,128,512]{2,1,0:T(8,128)} %all_to_all.21), kind=kOutput, calls=%fused_computation.5 | convolution fusion | flops 3221225472 | bytes 12713984 | tf_op jit(solution)/shard_map/dot_general | solution.py:25
  628.3 1.9 collective-permute-start
  630.3 9.2 %collective-permute-done = f32[128,256]{1,0:T(8,128)S(1)} collective-permute-done((f32[128,256]{1,0:T(8,128)S(1)}, f32[128,256]{1,0:T(8,128)S(1)}, u32[]{:S(2)}, u32[]{:S(2)}) %collective-permute-start) | collective-permute-done | bytes 131104 | tf_op jit(solution)/shard_map/ppermute | solution.py:9
  639.5 0.8 gather_fusion
  640.2 0.1 broadcast_select_fusion
  640.3 0.1 copy.5
  640.4 0.7 gather_fusion.1
  641.1 0.1 copy.6
  641.2 0.7 bitcast_add_fusion
  (4 shorter events, 0.0 us)
Async XLA Ops:
  0.0 193.0 %copy-start = (f32[256,512]{1,0:T(8,128)S(1)}, f32[256,512]{1,0:T(8,128)}, u32[]{:S(2)}) copy-start(f32[256,512]{1,0:T(8,128)} %param.4) | copy-start | bytes 1572868
  197.3 17.3 %copy-start.2 = (s32[128]{0:T(128)S(1)}, s32[128]{0:T(128)}, u32[]{:S(2)}) copy-start(s32[128]{0:T(128)} %param.7) | copy-start | bytes 1540
  197.3 17.4 %copy-start.1 = (s32[256]{0:T(256)S(1)}, s32[256]{0:T(256)}, u32[]{:S(2)}) copy-start(s32[256]{0:T(256)} %param.6) | copy-start | bytes 3076
  197.3 417.9 %all-to-all-start.1 = ((f32[16,256,512]{2,1,0:T(8,128)}), f32[16,256,512]{2,1,0:T(8,128)}, u32[]{:S(2)}, u32[]{:S(2)}) async-start(f32[16,256,512]{2,1,0:T(8,128)} %stack.2), calls=%async_computation.1 | async-start | bytes 16777216 | tf_op jit(solution)/shard_map/all_to_all | solution.py:21
  628.3 11.2 %collective-permute-start = (f32[128,256]{1,0:T(8,128)S(1)}, f32[128,256]{1,0:T(8,128)S(1)}, u32[]{:S(2)}, u32[]{:S(2)}) collective-permute-start(f32[128,256]{1,0:T(8,128)S(1)} %fusion.3), channel_id=1, source_target_pairs={{0,256},{16,272},{32,288},{48,304},{64,320},{80,336},{96,352},{112... | collective-permute-start | bytes 393224 | tf_op jit(solution)/shard_map/ppermute | solution.py:9
